TPU v7x, 256 devices: a whole 4x4x8 slice. The times are simulated.
256 devices in a mesh: req: 64 (over z, y, core), tp: 4 (over x).
Axes of the slice: x: 4, y: 4, z: 8, core: 2. Of those that a mesh axis runs over, the one named last changes fastest.
Arguments:
- hidden_in: bfloat16 [8192, 2048], P('req'), may hold values from -6 to 6
- attn_gain: float32 [2048], replicated, may hold values from 0.1 to 1.9
- w_query: bfloat16 [2048, 3072], P(None, 'tp'), may hold values from -0.125 to 0.125
- w_latent: bfloat16 [2048, 576], P(None, 'tp'), may hold values from -0.125 to 0.125
- kv_gain: float32 [512], replicated, may hold values from 0.1 to 1.9
- w_key_up: bfloat16 [512, 2048], P(None, 'tp'), may hold values from -0.25 to 0.25
- w_value_up: bfloat16 [512, 2048], P(None, 'tp'), may hold values from -0.25 to 0.25
- w_out: bfloat16 [2048, 2048], P('tp'), may hold values from -0.125 to 0.125
- moe_gain: float32 [2048], replicated, may hold values from 0.1 to 1.9
- w_gate: bfloat16 [64, 2048, 1408], P('req', None, 'tp'), may hold values from -0.125 to 0.125
- w_up: bfloat16 [64, 2048, 1408], P('req', None, 'tp'), may hold values from -0.125 to 0.125
- w_down: bfloat16 [64, 1408, 2048], P('req', 'tp'), may hold values from -0.15625 to 0.15625
- latent_cache: bfloat16 [2048, 64, 576], P('req'), may hold values from -3000 to 3000
- page_table: int32 [256, 8], P('req'), may hold values from 0 to 7, as said below
- cache_len: int32 [256], P('req'), may hold values from 1 to 512, 65536 in all
- parents: int32 [256, 3, 8], P('req'), may hold values from 0 to 7
- routes: int32 [8192, 6], P('req'), may hold values from 0 to 63, all different within a row; in each aligned block of 128 rows (0 to 127, 128 to 255, ...) at most 24 rows name the same one
- route_weights: float32 [8192, 6], P('req'), may hold values from 0.1 to 1
Outputs:
- layer_out: bfloat16 [8192, 2048], P('req', 'tp')
Inputs may be any that keep to these rules, and one draw needn't show every extreme that they name: `page_table`: each request's row lists the 8 pages of that request's block of the pool, each once. `routes`: each row names 6 different experts; in the rows of one index of req no expert is named more than 24 times, a bound that some block reaches.
All inputs are finite; a program needn't handle non-finite values. No bound on the sum of `cache_len` on one device may be relied on, other than what follows from the above.
Results may differ from a plain program's by a relative error of at most 0.015.
The roundings to bfloat16 on the way count: a program that leaves them out, or rounds other values in their place, can miss the bound.
Values may be sent and summed in bfloat16 or wider, within the bound.
No kernel may reach another device: no remote copies, remote signals or barrier semaphores. Data moves between devices by JAX's collectives and lax.ppermute only.
A program may use at most 128 MiB of HBM per device.

v0:
```python
import jax
import jax.numpy as jnp
from jax import lax
from jax.sharding import PartitionSpec as P

D = 2048
NOPE = 128
ROPE = 64
VDIM = 128
LATENT = 512
TOPK = 6
EXP_DEV = 1
BEAMS = 8
STEPS = 4
PAGE = 64
PAGES = 8
eps = 1e-06
rope_base = 50000.0


def rms_scale(values):
    return lax.rsqrt(jnp.mean(values * values, axis=-1, keepdims=True) + eps)


def rotate(values, cos_val, sin_val):
    half_rope = values.shape[-1] // 2
    first = values[..., :half_rope]
    second = values[..., half_rope:]
    return jnp.concatenate(
        [first * cos_val - second * sin_val, second * cos_val + first * sin_val], axis=-1
    )


def expert_math(arrived, gate_w, up_w, down_w):
    gate_val = jnp.einsum("nesd,edf->nesf", arrived, gate_w, preferred_element_type=jnp.float32)
    up_val = jnp.einsum("nesd,edf->nesf", arrived, up_w, preferred_element_type=jnp.float32)
    active = (jax.nn.silu(gate_val) * up_val).astype(jnp.bfloat16)
    return jnp.einsum("nesf,efd->nesd", active, down_w, preferred_element_type=jnp.float32)


def send_home(shares):
    return lax.all_to_all(shares, "req", split_axis=0, concat_axis=0, tiled=True)


def local(
    hidden_in,
    attn_gain,
    w_query,
    w_latent,
    kv_gain,
    w_key_up,
    w_value_up,
    w_out,
    moe_gain,
    w_gate,
    w_up,
    w_down,
    latent_cache,
    page_table,
    cache_len,
    parents,
    routes,
    route_weights,
):
    highest = lax.Precision.HIGHEST
    row_count = hidden_in.shape[0]
    req_local = cache_len.shape[0]
    heads_local = w_value_up.shape[1] // VDIM
    tp_count = lax.axis_size("tp")
    req_count = lax.axis_size("req")
    col_share = D // tp_count
    max_len = PAGES * PAGE
    hidden_f = hidden_in.astype(jnp.float32)
    normed = (hidden_f * rms_scale(hidden_f) * attn_gain).astype(jnp.bfloat16)
    positions = (
        cache_len.astype(jnp.float32)[:, None, None]
        + jnp.arange(STEPS, dtype=jnp.float32)[None, :, None]
        + jnp.zeros((1, 1, BEAMS), jnp.float32)
    ).reshape(row_count)
    frequency = rope_base ** (-2.0 * jnp.arange(ROPE // 2, dtype=jnp.float32) / ROPE)
    angles = positions[:, None] * frequency[None, :]
    cos_val = jnp.cos(angles)
    sin_val = jnp.sin(angles)
    queries = jnp.dot(normed, w_query, preferred_element_type=jnp.float32).reshape(
        row_count, heads_local, NOPE + ROPE
    )
    q_nope = queries[:, :, :NOPE].astype(jnp.bfloat16)
    q_rope = rotate(queries[:, :, NOPE:], cos_val[:, None, :], sin_val[:, None, :]).astype(
        jnp.bfloat16
    )
    kv_part = jnp.dot(normed, w_latent, preferred_element_type=jnp.float32)
    kv_all = lax.all_gather(kv_part, "tp", axis=1, tiled=True)
    new_lat = kv_all[:, :LATENT] * rms_scale(kv_all[:, :LATENT]) * kv_gain
    new_rope = rotate(kv_all[:, LATENT:], cos_val, sin_val)
    new_keys = jnp.concatenate([new_lat, new_rope], axis=1).astype(jnp.bfloat16)
    key_up = w_key_up.reshape(LATENT, heads_local, NOPE)
    q_lat = jnp.einsum("nhc,lhc->nhl", q_nope, key_up, preferred_element_type=jnp.float32).astype(
        jnp.bfloat16
    )
    query_key = jnp.concatenate([q_lat, q_rope], axis=2)
    pool_index = (jnp.arange(req_local, dtype=jnp.int32) * PAGES)[:, None] + page_table
    cache_keys = jnp.take(latent_cache, pool_index.reshape(-1), axis=0).reshape(
        req_local, max_len, LATENT + ROPE
    )
    live_mask = jnp.arange(max_len, dtype=jnp.int32)[None, :] < cache_len[:, None]
    score_scale = (NOPE + ROPE) ** (-0.5)
    grouped = query_key.reshape(req_local, STEPS * BEAMS * heads_local, LATENT + ROPE)
    s_cache = (
        jnp.einsum("rqd,rld->rql", grouped, cache_keys, preferred_element_type=jnp.float32)
        * score_scale
    )
    s_cache = jnp.where(live_mask[:, None, :], s_cache, -jnp.inf).reshape(
        req_local, STEPS, BEAMS, heads_local, max_len
    )
    fresh = new_keys.reshape(req_local, STEPS, BEAMS, LATENT + ROPE).astype(jnp.float32)
    parent_hot = (parents[..., None] == jnp.arange(BEAMS, dtype=jnp.int32)).astype(jnp.float32)
    identity = jnp.broadcast_to(jnp.eye(BEAMS, dtype=jnp.float32), (req_local, BEAMS, BEAMS))
    tail_rows = []
    for step_index in range(STEPS):
        lineage = identity
        pieces = [None] * STEPS
        for earlier in range(step_index, -1, -1):
            pieces[earlier] = jnp.einsum(
                "rba,rad->rbd", lineage, fresh[:, earlier], precision=highest
            )
            if earlier > 0:
                lineage = jnp.einsum(
                    "rba,rac->rbc", lineage, parent_hot[:, earlier - 1], precision=highest
                )
        for later in range(step_index + 1, STEPS):
            pieces[later] = jnp.zeros_like(pieces[0])
        tail_rows.append(jnp.stack(pieces, axis=2))
    tail_keys = jnp.stack(tail_rows, axis=1).astype(jnp.bfloat16)
    queries_tail = query_key.reshape(req_local, STEPS, BEAMS, heads_local, LATENT + ROPE)
    s_tail = (
        jnp.einsum(
            "rsbhd,rsbjd->rsbhj", queries_tail, tail_keys, preferred_element_type=jnp.float32
        )
        * score_scale
    )
    causal = jnp.arange(STEPS)[None, :] <= jnp.arange(STEPS)[:, None]
    s_tail = jnp.where(causal[None, :, None, None, :], s_tail, -jnp.inf)
    top_score = jnp.maximum(jnp.max(s_cache, axis=-1), jnp.max(s_tail, axis=-1))
    e_cache = jnp.exp(s_cache - top_score[..., None])
    e_tail = jnp.exp(s_tail - top_score[..., None])
    total = jnp.sum(e_cache, axis=-1) + jnp.sum(e_tail, axis=-1)
    p_cache = (e_cache / total[..., None]).astype(jnp.bfloat16)
    p_tail = (e_tail / total[..., None]).astype(jnp.bfloat16)
    context = jnp.einsum(
        "rsbhl,rld->rsbhd", p_cache, cache_keys[..., :LATENT], preferred_element_type=jnp.float32
    )
    context = context + jnp.einsum(
        "rsbhj,rsbjd->rsbhd", p_tail, tail_keys[..., :LATENT], preferred_element_type=jnp.float32
    )
    context = context.astype(jnp.bfloat16).reshape(row_count, heads_local, LATENT)
    value_up = w_value_up.reshape(LATENT, heads_local, VDIM)
    head_out = (
        jnp.einsum("nhl,lhv->nhv", context, value_up, preferred_element_type=jnp.float32)
        .astype(jnp.bfloat16)
        .reshape(row_count, heads_local * VDIM)
    )
    attn_part = jnp.dot(head_out, w_out, preferred_element_type=jnp.float32)
    expert_count = EXP_DEV * req_count
    capacity = min(row_count, 2 * row_count * TOPK // expert_count)
    slot_count = expert_count * capacity
    picks = routes.reshape(-1)
    pick_hot = (picks[:, None] == jnp.arange(expert_count, dtype=jnp.int32)[None, :]).astype(
        jnp.int32
    )
    before = jnp.cumsum(pick_hot, axis=0) - pick_hot
    ranks = jnp.sum(before * pick_hot, axis=1)
    slot_of = picks * capacity + ranks
    slot_hot = (slot_of[:, None] == jnp.arange(slot_count, dtype=jnp.int32)[None, :]).reshape(
        row_count, TOPK, slot_count
    )
    gather_rows = jnp.sum(slot_hot.astype(jnp.int32), axis=1).astype(jnp.bfloat16)
    weight_rows = jnp.sum(jnp.where(slot_hot, route_weights[:, :, None], 0.0), axis=1)
    tp_index = lax.axis_index("tp")
    col_start = tp_index * col_share
    attn_full = lax.psum(attn_part, "tp")
    resid_full = hidden_f + attn_full
    moe_in = (resid_full * rms_scale(resid_full) * moe_gain).astype(jnp.bfloat16)
    placed = jnp.dot(gather_rows.T, moe_in, preferred_element_type=jnp.float32).astype(jnp.bfloat16)
    partial_out = expert_math(
        lax.all_to_all(
            placed.reshape(req_count, EXP_DEV, capacity, moe_in.shape[1]),
            "req",
            split_axis=0,
            concat_axis=0,
            tiled=True,
        ),
        w_gate,
        w_up,
        w_down,
    )
    shares = lax.psum_scatter(partial_out, "tp", scatter_dimension=3, tiled=True)
    returned = send_home(shares.astype(jnp.bfloat16))
    resid_cols = lax.dynamic_slice_in_dim(resid_full, col_start, col_share, 1)
    combined = jnp.dot(
        weight_rows, returned.reshape(slot_count, col_share).astype(jnp.float32), precision=highest
    )
    return (resid_cols + combined).astype(jnp.bfloat16)


def solution(mesh):
    in_specs = (
        P("req", None),
        P(),
        P(None, "tp"),
        P(None, "tp"),
        P(),
        P(None, "tp"),
        P(None, "tp"),
        P("tp", None),
        P(),
        P("req", None, "tp"),
        P("req", None, "tp"),
        P("req", "tp", None),
        P("req", None, None),
        P("req", None),
        P("req"),
        P("req", None, None),
        P("req", None),
        P("req", None),
    )
    out_specs = P("req", "tp")
    return jax.shard_map(local, mesh=mesh, in_specs=in_specs, out_specs=out_specs, check_vma=False)
```

profile of v0, /device:TPU:1, one launch (start us, length us, event | category | flops | bytes accessed | tf_op | source)
XLA Modules:
  0.0 477.5 jit_solution(17207747423116017685)
XLA Ops:
  7.1 0.8 iota_compare_fusion.3
  8.2 1.2 fusion.40
  9.5 1.6 fusion.63
  11.1 11.2 %all_gather.3 = f32[128,576]{0,1:T(8,128)S(1)} all-gather(f32[128,144]{0,1:T(8,128)S(1)} %fusion.63), channel_id=1, replica_groups=mesh['req'=64,'tp'=4] {'tp'}, dimensions={1}, use_global_device_ids=true | all-gather | bytes 368640 | tf_op jit(solution)/shard_map/all_gather | solution.py:92
  22.4 0.8 multiply_convert_fusion.2
  23.2 1.6 copy.150
  25.1 0.8 multiply_cosine_fusion
  26.4 1.0 pad_maximum_fusion.2
  27.4 0.8 fusion.37
  28.3 0.8 fusion.34
  29.1 0.8 fusion.38
  30.1 0.8 fusion.30
  30.9 0.8 fusion.32
  31.6 0.8 fusion.35
  32.4 0.8 fusion.39
  35.0 0.8 fusion.36
  35.8 0.8 fusion.33
  36.6 0.8 fusion.31
  38.8 2.4 fusion.65
  41.5 1.4 fusion.22
  42.9 0.9 subtract_convert_fusion
  44.5 1.2 reshape.300
  46.0 4.1 gather_fusion
  50.1 2.1 bitcast_select_fusion
  52.3 2.0 fusion.86
  54.5 0.9 maximum_bitcast_fusion
  55.6 3.1 fusion.87
  59.0 1.2 fusion.58
  60.2 2.6 reshape.302
  62.8 1.5 exponential_reduce_fusion
  64.6 1.7 fusion.51
  66.3 0.9 fusion.21
  67.3 1.4 copy.179
  69.1 1.5 fusion.88
  71.2 1.8 reduce-window.6
  74.4 50.8 %all-reduce.2.cloned.1.call-done = f32[128,2048]{1,0:T(8,128)} async-done(((f32[128,2048]{1,0:T(8,128)}), f32[128,2048]{1,0:T(8,128)}) %all-reduce.2.cloned.1.call-update) | async-done | bytes 1048592 | tf_op jit(solution)/shard_map/psum | solution.py:180
  125.1 1.4 multiply_reduce_fusion
  126.6 1.9 convolution_convert_fusion
  128.5 151.6 %all_to_all.10 = bf16[64,1,24,2048]{3,2,1,0:T(8,128)(2,1)S(1)} all-to-all(bf16[64,1,24,2048]{3,2,1,0:T(8,128)(2,1)S(1)} %bitcast.216), channel_id=1, replica_groups=mesh['req'=64,'tp'=4] {'req'}, dimensions={0} | all-to-all | bytes 12582912 | tf_op jit(solution)/shard_map/all_to_all | solution.py:185
  280.1 2.6 copy-done.2
  282.6 5.0 %fusion.2 = f32[64,24,352]{2,1,0:T(8,128)} fusion(bf16[64,1,24,2048]{3,2,1,0:T(8,128)(2,1)S(1)} %all_to_all.10, bf16[1,2048,352]{1,2,0:T(8,128)(2,1)S(1)} %copy-done.25), kind=kOutput, calls=%fused_computation.4 | convolution fusion | flops 2214592512 | bytes 9895936 | tf_op jit(solution)/shard_map/nesd,edf->nesf/dot_general | solution.py:35
  287.7 12.3 %convolution_bitcast_fusion = f32[64,1,24,2048]{3,2,0,1:T(8,128)} fusion(bf16[1,352,2048]{2,1,0:T(8,128)(2,1)S(1)} %copy-done.26, bf16[1,2048,352]{1,2,0:T(8,128)(2,1)} %param.28, bf16[64,1,24,2048]{3,2,1,0:T(8,128)(2,1)} %copy-done.2, f32[64,24,352]{2,1,0:T(8,128)} %fusion.2), kind=kOutput, calls=%fused_computation.6 | convolution fusion | flops 4432429056 | bytes 23920640 | tf_op jit(solution)/shard_map/nesf,efd->nesd/dot_general | solution.py:38
  300.0 114.4 %reduce-scatter.2.cloned.1.call-done = f32[64,1,24,512]{3,2,0,1:T(8,128)} async-done(((f32[64,1,24,2048]{3,2,0,1:T(8,128)}), f32[64,1,24,512]{3,2,0,1:T(8,128)}) %reduce-scatter.2.cloned.1.call-update) | async-done | bytes 3145744 | tf_op jit(solution)/shard_map/reduce_scatter | solution.py:196
  414.4 3.2 convert_bitcast_fusion
  417.7 10.9 %all-to-all-start.1 = ((bf16[64,1,24,512]{3,2,1,0:T(8,128)(2,1)}), bf16[64,1,24,512]{3,2,1,0:T(8,128)(2,1)}, u32[]{:S(2)}, u32[]{:S(2)}) async-start(bf16[64,1,24,512]{3,2,1,0:T(8,128)(2,1)} %convert_bitcast_fusion), calls=%async_computation.2 | async-start | bytes 3145728 | tf_op jit(solution)/shard_map/all_to_all | solution.py:42
  428.6 1.5 select_reduce_fusion
  430.2 37.4 %all-to-all-done.1 = bf16[64,1,24,512]{3,2,1,0:T(8,128)(2,1)} async-done(((bf16[64,1,24,512]{3,2,1,0:T(8,128)(2,1)}), bf16[64,1,24,512]{3,2,1,0:T(8,128)(2,1)}, u32[]{:S(2)}, u32[]{:S(2)}) %all-to-all-start.1) | async-done | bytes 1572896 | tf_op jit(solution)/shard_map/all_to_all | solution.py:42
  467.6 3.1 fusion.29
  (120 shorter events, 9.7 us)
Async XLA Ops:
  6.5 32.2 %copy-start = (bf16[2048,768]{1,0:T(8,128)(2,1)S(1)}, bf16[2048,768]{1,0:T(8,128)(2,1)}, u32[]{:S(2)}) copy-start(bf16[2048,768]{1,0:T(8,128)(2,1)} %param.20) | copy-start | bytes 9437188
  6.5 15.8 %copy-start.21 = (f32[512]{0:T(512)S(1)}, f32[512]{0:T(512)}, u32[]{:S(2)}) copy-start(f32[512]{0:T(512)} %param.22) | copy-start | bytes 6148
  6.5 18.3 %copy-start.23 = (s32[4]{0:T(128)S(1)}, s32[4]{0:T(128)}, u32[]{:S(2)}) copy-start(s32[4]{0:T(128)} %param.32) | copy-start | bytes 52
  6.5 118.6 %all-reduce.2.cloned.1.call-start = ((), (), s32[]{:S(2)}) async-start(), calls=%async_computation.3 | async-start | bytes 2097152 | tf_op jit(solution)/shard_map/psum | solution.py:180
  9.5 29.3 %copy-start.18 = (f32[2048]{0:T(1024)S(1)}, f32[2048]{0:T(1024)}, u32[]{:S(2)}) copy-start(f32[2048]{0:T(1024)} %param.19) | copy-start | bytes 24580
  42.9 2.8 copy-start.22
  42.9 2.8 copy-start.24
  44.0 6.1 %copy-start.6 = (bf16[128,4,576]{2,0,1:T(8,128)(2,1)}, bf16[128,4,576]{2,0,1:T(8,128)(2,1)S(1)}, u32[]{:S(2)}) copy-start(bf16[128,4,576]{2,0,1:T(8,128)(2,1)S(1)} %pad_maximum_fusion) | copy-start | bytes 1769476
  50.1 2.1 copy-start.5
  52.2 2.3 copy-start.10
  52.2 2.3 copy-start.11
  52.2 2.3 copy-start.12
  52.2 2.3 copy-start.13
  52.2 2.3 copy-start.14
  52.2 2.3 copy-start.15
  52.3 2.3 copy-start.16
  54.3 1.4 copy-start.27
  55.6 3.1 copy-start.7
  58.7 5.9 %slice-start = ((bf16[4,4,8,4,576]{4,2,0,3,1:T(8,128)(2,1)}), bf16[4,4,8,4,512]{4,2,0,3,1:T(8,128)(2,1)S(1)}, s32[]{:S(2)}) async-start(bf16[4,4,8,4,576]{4,2,0,3,1:T(8,128)(2,1)} %copy-done.7), calls=%async_computation.5 | async-start | bytes 1048576 | tf_op jit(solution)/shard_map/slice | solution.py:153
  64.6 1.7 copy-start.9
  67.3 1.8 copy-start.8
  69.0 1.8 copy-start.17
  70.5 54.6 %copy-start.4 = (bf16[128,2048]{1,0:T(8,128)(2,1)S(1)}, bf16[128,2048]{1,0:T(8,128)(2,1)}, u32[]{:S(2)}) copy-start(bf16[128,2048]{1,0:T(8,128)(2,1)} %param.18) | copy-start | bytes 1572868
  70.6 343.9 %reduce-scatter.2.cloned.1.call-start = ((), (), s32[]{:S(2)}) async-start(), calls=%async_computation.4 | async-start | bytes 15728640 | tf_op jit(solution)/shard_map/reduce_scatter | solution.py:196
  70.9 55.7 %copy-start.19 = (f32[2048]{0:T(1024)S(1)}, f32[2048]{0:T(1024)}, u32[]{:S(2)}) copy-start(f32[2048]{0:T(1024)} %param.26) | copy-start | bytes 24580
  126.6 1.9 copy-start.3
  128.5 154.2 %copy-start.25 = (bf16[1,2048,352]{1,2,0:T(8,128)(2,1)S(1)}, bf16[1,2048,352]{1,2,0:T(8,128)(2,1)}, u32[]{:S(2)}) copy-start(bf16[1,2048,352]{1,2,0:T(8,128)(2,1)} %param.27) | copy-start | bytes 4325380
  280.1 2.6 copy-start.2
  282.6 5.0 %copy-start.26 = (bf16[1,352,2048]{2,1,0:T(8,128)(2,1)S(1)}, bf16[1,352,2048]{2,1,0:T(8,128)(2,1)}, u32[]{:S(2)}) copy-start(bf16[1,352,2048]{2,1,0:T(8,128)(2,1)} %param.29) | copy-start | bytes 4325380
  417.7 11.0 %copy-start.20 = (f32[128,6]{0,1:T(8,128)S(1)}, f32[128,6]{0,1:T(8,128)}, u32[]{:S(2)}) copy-start(f32[128,6]{0,1:T(8,128)} %param.35) | copy-start | bytes 9220
  417.7 49.9 %all-to-all-start.1 = ((bf16[64,1,24,512]{3,2,1,0:T(8,128)(2,1)}), bf16[64,1,24,512]{3,2,1,0:T(8,128)(2,1)}, u32[]{:S(2)}, u32[]{:S(2)}) async-start(bf16[64,1,24,512]{3,2,1,0:T(8,128)(2,1)} %convert_bitcast_fusion), calls=%async_computation.2 | async-start | bytes 3145728 | tf_op jit(solution)/shard_map/all_to_all | solution.py:42
  428.6 42.1 %copy-start.1 = (bf16[2048,768]{1,0:T(8,128)(2,1)S(1)}, bf16[2048,768]{1,0:T(8,128)(2,1)}, u32[]{:S(2)}) copy-start(bf16[2048,768]{1,0:T(8,128)(2,1)} %param.20) | copy-start | bytes 9437188
Sparse Core Ops, SparseCore 0:
  70.7 54.3 all-reduce.1
  300.1 114.2 reduce-scatter.1
where the time goes:
time: 478 us
  waiting for transfers between devices  203 us (42%)
  blocking collectives  163 us (34%)
  matrix products  45.9 us (10%)
  other arithmetic  23 us (5%)
  local copies, waits for them, and re-layouts  18.1 us (4%)
  between operations  14 us (3%)
  starting transfers between devices  11.2 us (2%)
    all_to_all x1, blocking collectives, local(): lax.all_to_all(placed.reshape(req_count, EXP_DEV, capacity, moe_in.shape[...  152 us
    reduce_scatter x1, waiting for transfers between devices, local(): lax.psum_scatter(partial_out, 'tp', scatter_dimension=3, tiled=True)  114 us
    psum x1, waiting for transfers between devices, local(): attn_full = lax.psum(attn_part, 'tp')  50.8 us
    all_to_all x1, waiting for transfers between devices, send_home(): lax.all_to_all(shares, 'req', split_axis=0, concat_axis=0, tiled=True)  37.4 us
    dot_general x1, matrix products, expert_math(): jnp.einsum('nesf,efd->nesd', active, down_w, preferred_element_type=jnp.f...  12.3 us
    all_gather x1, blocking collectives, local(): kv_all = lax.all_gather(kv_part, 'tp', axis=1, tiled=True)  11.2 us
    all_to_all x1, starting transfers between devices, send_home(): lax.all_to_all(shares, 'req', split_axis=0, concat_axis=0, tiled=True)  10.9 us
  transfers between devices with their start and end apart: 3, of which 3 were waited for; matrix products, arithmetic and copies ran while one was open for 1% of the time, Pallas kernels for 0%

commit v1 on v0

--- a/solution.py
+++ b/solution.py
@@ -16,6 +16,16 @@
 PAGES = 8
 eps = 1e-06
 rope_base = 50000.0
+
+
+def pass_along(x, axis, along):
+    count = lax.axis_size(axis)
+    held, pieces = (x, [x])
+    for _ in range(count - 1):
+        held = lax.ppermute(held, axis, [(i, (i + 1) % count) for i in range(count)])
+        pieces.insert(0, held)
+    line = jnp.concatenate(pieces, axis=along)
+    return jnp.roll(line, (lax.axis_index(axis) + 1) * x.shape[along], axis=along)
 
 
 def rms_scale(values):
@@ -89,7 +99,7 @@
         jnp.bfloat16
     )
     kv_part = jnp.dot(normed, w_latent, preferred_element_type=jnp.float32)
-    kv_all = lax.all_gather(kv_part, "tp", axis=1, tiled=True)
+    kv_all = pass_along(kv_part, "tp", 1)
     new_lat = kv_all[:, :LATENT] * rms_scale(kv_all[:, :LATENT]) * kv_gain
     new_rope = rotate(kv_all[:, LATENT:], cos_val, sin_val)
     new_keys = jnp.concatenate([new_lat, new_rope], axis=1).astype(jnp.bfloat16)

time: 478 us -> 481 us (level)
  blocking collectives: 163 us -> 152 us
  local copies, waits for them, and re-layouts: 18.1 us -> 24.1 us
  waiting for transfers between devices: 203 us -> 209 us
    all_gather x1 -> x0, blocking collectives: 11.2 us -> none  [local(): kv_all = lax.all_gather(kv_part, 'tp', axis=1, tiled=True)]
    ppermute x0 -> x3, waiting for transfers between devices: none -> 7.6 us  [pass_along(): lax.ppermute(held, axis, [(i, (i + 1) % count) for i in range(count)])]
  transfers between devices with their start and end apart: 3 -> 6, of which waited for: 3 -> 5; matrix products, arithmetic and copies ran while one was open for 1% -> 5% of each run, Pallas kernels for 0% -> 0%
where the time goes in v1:
time: 481 us; the launch traced here: 480 us
  waiting for transfers between devices  209 us (43%)
  blocking collectives  152 us (32%)
  matrix products  45.1 us (9%)
  local copies, waits for them, and re-layouts  24.1 us (5%)
  other arithmetic  22.3 us (5%)
  starting transfers between devices  14.3 us (3%)
  between operations  13.9 us (3%)
    all_to_all x1, blocking collectives, local(): lax.all_to_all(placed.reshape(req_count, EXP_DEV, capacity, moe_in.shape[...  152 us
    reduce_scatter x1, waiting for transfers between devices, local(): lax.psum_scatter(partial_out, 'tp', scatter_dimension=3, tiled=True)  114 us
    psum x1, waiting for transfers between devices, local(): attn_full = lax.psum(attn_part, 'tp')  49.1 us
    all_to_all x1, waiting for transfers between devices, send_home(): lax.all_to_all(shares, 'req', split_axis=0, concat_axis=0, tiled=True)  37.4 us
    dot_general x1, matrix products, expert_math(): jnp.einsum('nesf,efd->nesd', active, down_w, preferred_element_type=jnp.f...  12.3 us
    all_to_all x1, starting transfers between devices, send_home(): lax.all_to_all(shares, 'req', split_axis=0, concat_axis=0, tiled=True)  10.9 us
  transfers between devices with their start and end apart: 6, of which 5 were waited for; matrix products, arithmetic and copies ran while one was open for 5% of the time, Pallas kernels for 0%

profile of v1, /device:TPU:1, one launch (start us, length us, event | category | flops | bytes accessed | tf_op | source)
XLA Modules:
  0.0 480.0 jit_solution(17984528509107629074)
XLA Ops:
  6.5 1.4 fusion.40
  7.9 1.6 fusion.63
  9.6 2.1 collective-permute-start
  14.9 2.1 fusion.65
  19.4 4.1 gather_fusion
  23.5 2.0 bitcast_select_fusion
  25.7 0.8 copy.180
  26.6 0.8 copy.181
  27.4 2.1 copy.179
  29.5 1.2 collective-permute-start.1
  30.8 3.2 collective-permute-done.1
  34.0 4.4 collective-permute-done.2
  39.5 1.6 multiply_cosine_fusion
  42.0 0.8 pad_maximum_fusion.2
  43.0 0.9 fusion.34
  43.9 0.8 fusion.38
  44.7 0.8 fusion.30
  45.5 0.8 fusion.32
  47.8 0.8 copy.144
  48.6 0.8 copy.146
  49.5 1.1 subtract_convert_fusion
  50.7 0.9 copy-done.6
  51.5 1.3 copy.147
  52.9 2.2 reshape.300
  55.1 3.1 fusion.86
  58.9 1.0 maximum_bitcast_fusion
  60.1 3.1 fusion.87
  63.4 1.2 fusion.58
  64.6 2.6 reshape.302
  67.2 1.5 exponential_reduce_fusion
  69.0 1.7 fusion.51
  70.8 0.9 fusion.21
  72.1 1.2 copy-done.8
  73.3 1.5 fusion.88
  75.3 1.8 reduce-window.6
  78.4 49.1 %all-reduce.2.cloned.1.call-done = f32[128,2048]{1,0:T(8,128)} async-done(((f32[128,2048]{1,0:T(8,128)}), f32[128,2048]{1,0:T(8,128)}) %all-reduce.2.cloned.1.call-update) | async-done | bytes 1048592 | tf_op jit(solution)/shard_map/psum | solution.py:190
  127.6 1.4 multiply_reduce_fusion
  129.0 1.9 convolution_convert_fusion
  130.9 151.6 %all_to_all.10 = bf16[64,1,24,2048]{3,2,1,0:T(8,128)(2,1)S(1)} all-to-all(bf16[64,1,24,2048]{3,2,1,0:T(8,128)(2,1)S(1)} %bitcast.216), channel_id=1, replica_groups=mesh['req'=64,'tp'=4] {'req'}, dimensions={0} | all-to-all | bytes 12582912 | tf_op jit(solution)/shard_map/all_to_all | solution.py:195
  282.5 2.6 copy-done.2
  285.1 5.0 %fusion.2 = f32[64,24,352]{2,1,0:T(8,128)} fusion(bf16[64,1,24,2048]{3,2,1,0:T(8,128)(2,1)S(1)} %all_to_all.10, bf16[1,2048,352]{1,2,0:T(8,128)(2,1)S(1)} %copy-done.23), kind=kOutput, calls=%fused_computation.4 | convolution fusion | flops 2214592512 | bytes 9895936 | tf_op jit(solution)/shard_map/nesd,edf->nesf/dot_general | solution.py:45
  290.1 12.3 %convolution_bitcast_fusion = f32[64,1,24,2048]{3,2,0,1:T(8,128)} fusion(bf16[1,352,2048]{2,1,0:T(8,128)(2,1)S(1)} %copy-done.24, bf16[1,2048,352]{1,2,0:T(8,128)(2,1)} %param.28, bf16[64,1,24,2048]{3,2,1,0:T(8,128)(2,1)} %copy-done.2, f32[64,24,352]{2,1,0:T(8,128)} %fusion.2), kind=kOutput, calls=%fused_computation.6 | convolution fusion | flops 4432429056 | bytes 23920640 | tf_op jit(solution)/shard_map/nesf,efd->nesd/dot_general | solution.py:48
  302.4 114.4 %reduce-scatter.2.cloned.1.call-done = f32[64,1,24,512]{3,2,0,1:T(8,128)} async-done(((f32[64,1,24,2048]{3,2,0,1:T(8,128)}), f32[64,1,24,512]{3,2,0,1:T(8,128)}) %reduce-scatter.2.cloned.1.call-update) | async-done | bytes 3145744 | tf_op jit(solution)/shard_map/reduce_scatter | solution.py:206
  416.9 3.2 convert_bitcast_fusion
  420.1 10.9 %all-to-all-start.1 = ((bf16[64,1,24,512]{3,2,1,0:T(8,128)(2,1)}), bf16[64,1,24,512]{3,2,1,0:T(8,128)(2,1)}, u32[]{:S(2)}, u32[]{:S(2)}) async-start(bf16[64,1,24,512]{3,2,1,0:T(8,128)(2,1)} %convert_bitcast_fusion), calls=%async_computation.2 | async-start | bytes 3145728 | tf_op jit(solution)/shard_map/all_to_all | solution.py:52
  431.1 1.5 select_reduce_fusion
  432.6 37.4 %all-to-all-done.1 = bf16[64,1,24,512]{3,2,1,0:T(8,128)(2,1)} async-done(((bf16[64,1,24,512]{3,2,1,0:T(8,128)(2,1)}), bf16[64,1,24,512]{3,2,1,0:T(8,128)(2,1)}, u32[]{:S(2)}, u32[]{:S(2)}) %all-to-all-start.1) | async-done | bytes 1572896 | tf_op jit(solution)/shard_map/all_to_all | solution.py:52
  470.0 3.1 fusion.29
  (127 shorter events, 13.2 us)
Async XLA Ops:
  6.5 8.4 %copy-start = (bf16[2048,768]{1,0:T(8,128)(2,1)S(1)}, bf16[2048,768]{1,0:T(8,128)(2,1)}, u32[]{:S(2)}) copy-start(bf16[2048,768]{1,0:T(8,128)(2,1)} %param.20) | copy-start | bytes 9437188
  6.5 121.0 %all-reduce.2.cloned.1.call-start = ((), (), s32[]{:S(2)}) async-start(), calls=%async_computation.3 | async-start | bytes 2097152 | tf_op jit(solution)/shard_map/psum | solution.py:190
  6.5 8.4 %copy-start.4 = (bf16[128,2048]{1,0:T(8,128)(2,1)S(1)}, bf16[128,2048]{1,0:T(8,128)(2,1)}, u32[]{:S(2)}) copy-start(bf16[128,2048]{1,0:T(8,128)(2,1)} %param.18) | copy-start | bytes 1572868
  9.6 7.4 %copy-start.12 = (bf16[512,512]{1,0:T(8,128)(2,1)S(1)}, bf16[512,512]{1,0:T(8,128)(2,1)}, u32[]{:S(2)}) copy-start(bf16[512,512]{1,0:T(8,128)(2,1)} %param.23) | copy-start | bytes 1572868
  9.6 19.9 %collective-permute-start = (f32[128,144]{0,1:T(8,128)S(1)}, f32[128,144]{0,1:T(8,128)S(1)}, u32[]{:S(2)}, u32[]{:S(2)}) collective-permute-start(f32[128,144]{0,1:T(8,128)S(1)} %fusion.63), channel_id=1, source_target_pairs={{0,1},{1,2},{2,3},{3,0},{4,5},{5,6},{6,7},{7,4},{8,9},{9,10},{10,1... | collective-permute-start | bytes 221192 | tf_op jit(solution)/shard_map/ppermute | solution.py:25
  14.1 4.5 copy-start.14
  14.9 2.5 copy-start.22
  25.5 13.8 %copy-start.21 = (f32[512]{0:T(512)S(1)}, f32[512]{0:T(512)}, u32[]{:S(2)}) copy-start(f32[512]{0:T(512)} %param.22) | copy-start | bytes 6148
  29.5 4.4 collective-permute-start.1
  33.9 4.4 collective-permute-start.2
  38.5 0.8 copy-start.11
  50.7 0.9 copy-start.6
  55.1 3.2 copy-start.17
  55.1 3.4 copy-start.16
  55.1 3.6 copy-start.15
  55.1 3.8 copy-start.13
  60.0 3.1 copy-start.7
  63.1 5.9 %slice-start = ((bf16[4,4,8,4,576]{4,2,0,3,1:T(8,128)(2,1)}), bf16[4,4,8,4,512]{4,2,0,3,1:T(8,128)(2,1)S(1)}, s32[]{:S(2)}) async-start(bf16[4,4,8,4,576]{4,2,0,3,1:T(8,128)(2,1)} %copy-done.7), calls=%async_computation.5 | async-start | bytes 1048576 | tf_op jit(solution)/shard_map/slice | solution.py:163
  69.0 1.7 copy-start.10
  70.8 1.0 copy-start.9
  71.7 1.6 copy-start.8
  72.1 2.8 copy-start.18
  74.8 52.8 %copy-start.5 = (bf16[128,2048]{1,0:T(8,128)(2,1)S(1)}, bf16[128,2048]{1,0:T(8,128)(2,1)}, u32[]{:S(2)}) copy-start(bf16[128,2048]{1,0:T(8,128)(2,1)} %param.18) | copy-start | bytes 1572868
  74.8 342.1 %reduce-scatter.2.cloned.1.call-start = ((), (), s32[]{:S(2)}) async-start(), calls=%async_computation.4 | async-start | bytes 15728640 | tf_op jit(solution)/shard_map/reduce_scatter | solution.py:206
  75.0 54.0 %copy-start.19 = (f32[2048]{0:T(1024)S(1)}, f32[2048]{0:T(1024)}, u32[]{:S(2)}) copy-start(f32[2048]{0:T(1024)} %param.26) | copy-start | bytes 24580
  129.0 1.9 copy-start.3
  130.9 154.2 %copy-start.23 = (bf16[1,2048,352]{1,2,0:T(8,128)(2,1)S(1)}, bf16[1,2048,352]{1,2,0:T(8,128)(2,1)}, u32[]{:S(2)}) copy-start(bf16[1,2048,352]{1,2,0:T(8,128)(2,1)} %param.27) | copy-start | bytes 4325380
  282.5 2.6 copy-start.2
  285.1 5.0 %copy-start.24 = (bf16[1,352,2048]{2,1,0:T(8,128)(2,1)S(1)}, bf16[1,352,2048]{2,1,0:T(8,128)(2,1)}, u32[]{:S(2)}) copy-start(bf16[1,352,2048]{2,1,0:T(8,128)(2,1)} %param.29) | copy-start | bytes 4325380
  420.1 11.0 %copy-start.20 = (f32[128,6]{0,1:T(8,128)S(1)}, f32[128,6]{0,1:T(8,128)}, u32[]{:S(2)}) copy-start(f32[128,6]{0,1:T(8,128)} %param.35) | copy-start | bytes 9220
  420.1 49.9 %all-to-all-start.1 = ((bf16[64,1,24,512]{3,2,1,0:T(8,128)(2,1)}), bf16[64,1,24,512]{3,2,1,0:T(8,128)(2,1)}, u32[]{:S(2)}, u32[]{:S(2)}) async-start(bf16[64,1,24,512]{3,2,1,0:T(8,128)(2,1)} %convert_bitcast_fusion), calls=%async_computation.2 | async-start | bytes 3145728 | tf_op jit(solution)/shard_map/all_to_all | solution.py:52
  431.1 42.1 %copy-start.1 = (bf16[2048,768]{1,0:T(8,128)(2,1)S(1)}, bf16[2048,768]{1,0:T(8,128)(2,1)}, u32[]{:S(2)}) copy-start(bf16[2048,768]{1,0:T(8,128)(2,1)} %param.20) | copy-start | bytes 9437188
Sparse Core Ops, SparseCore 0:
  74.9 52.5 all-reduce.1
  302.6 114.2 reduce-scatter.1
